TPU v7x, 32 devices: a whole 2x2x4 slice. The times are simulated.
32 devices in a mesh: img: 4 (over z), ref: 8 (over y, x, core).
Axes of the slice: x: 2, y: 2, z: 4, core: 2. Of those that a mesh axis runs over, the one named last changes fastest.
Arguments:
- images: bfloat16 [2048, 9216], P(('img', 'ref')), may hold values from -96 to 96
- references: bfloat16 [6912, 9216], P('ref'), may hold values from -0.5 to 0.5
- class_prior: float32 [192], P('ref'), may hold values from 0.2 to 5
Outputs:
- class_sums: float32 [192, 9216], P('ref', 'img')
- class_weights: float32 [192], P('ref')
All inputs are finite; a program needn't handle non-finite values.
Results may differ from a plain program's by a relative error of at most 0.0021.
Values may be sent and summed in bfloat16 or wider, within the bound.
No kernel may reach another device: no remote copies, remote signals or barrier semaphores. Data moves between devices by JAX's collectives and lax.ppermute only.
A program may use at most 128 MiB of HBM per device.

v0:
```python
import jax
import jax.numpy as jnp
from jax import lax
from jax.sharding import PartitionSpec as P

ANG = 144


def unturn(stacked, shift_size):
    classes_here, rotations, columns = stacked.shape
    cycles = stacked.reshape(classes_here, rotations, columns // ANG, ANG)
    doubled = jnp.concatenate([cycles, cycles], axis=3)
    result = doubled[:, 0, :, 0:ANG]
    for turn_index in range(1, rotations):
        start_col = turn_index * shift_size
        result = result + doubled[:, turn_index, :, start_col : start_col + ANG]
    return result.reshape(classes_here, columns)


def per_device(images, references, class_prior):
    local_refs, pixels = references.shape
    classes_here = class_prior.shape[0]
    rotations = local_refs // classes_here
    shift_size = ANG // rotations
    half_norm = 0.5 * jnp.einsum(
        "jp,jp->j", references, references, preferred_element_type=jnp.float32
    )
    offsets = (jnp.log(class_prior)[:, None] - half_norm.reshape(classes_here, rotations)).reshape(
        local_refs
    )
    gathered = lax.all_gather(images, "ref", axis=0, tiled=True)
    products = lax.dot_general(
        gathered, references, (((1,), (1,)), ((), ())), preferred_element_type=jnp.float32
    )
    scores = products + offsets
    local_max = jnp.max(scores, axis=1)
    top_score = lax.pmax(local_max, "ref")
    denominator = lax.psum(jnp.sum(jnp.exp(scores - top_score[:, None]), axis=1), "ref")
    weights = (jnp.exp(scores - top_score[:, None]) / denominator[:, None]).astype(jnp.bfloat16)
    local_mass = (
        jnp.sum(weights.astype(jnp.float32), axis=0).reshape(classes_here, rotations).sum(axis=1)
    )
    class_weights = lax.psum(local_mass, "img")
    sums = lax.dot_general(
        weights, gathered, (((0,), (0,)), ((), ())), preferred_element_type=jnp.float32
    )
    reduced = lax.psum_scatter(sums, "img", scatter_dimension=1, tiled=True)
    class_sums = unturn(reduced.reshape(classes_here, rotations, -1), shift_size)
    return (class_sums, class_weights)


def solution(mesh):
    placed = (P(("img", "ref"), None), P("ref", None), P("ref"))
    return jax.shard_map(
        per_device,
        mesh=mesh,
        in_specs=placed,
        out_specs=(P("ref", "img"), P("ref")),
        check_vma=False,
    )
```

profile of v0, /device:TPU:0, one launch (start us, length us, event | category | flops | bytes accessed | tf_op | source)
XLA Modules:
  0.0 719.0 jit_solution(10911316544609606139)
XLA Ops:
  8.8 7.0 fusion
  15.8 55.7 %all-gather.2.cloned.1.call-done = bf16[512,9216]{1,0:T(8,128)(2,1)} async-done(((bf16[64,9216]{1,0:T(8,128)(2,1)}), bf16[512,9216]{1,0:T(8,128)(2,1)}) %all-gather.2.cloned.1.call-update) | async-done | bytes 9437200 | tf_op jit(solution)/shard_map/all_gather | solution.py:31
  71.4 14.2 %add_reduce_fusion = (f32[512]{0:T(512)S(1)}, f32[512,864]{0,1:T(8,128)S(1)}) fusion(f32[864]{0:T(1024)S(1)} %multiply_subtract_fusion, bf16[512,9216]{1,0:T(8,128)(2,1)} %all-gather.2.cloned.1.call-done, bf16[864,9216]{1,0:T(8,128)(2,1)} %param.4), kind=kOutput, calls=%fused_computation.5 | convolution fusion | flops 8154611200 | bytes 27137408 | tf_op jit(solution)/shard_map/dot_general | solution.py:32
  85.6 13.1 %pmax.7 = f32[512]{0:T(512)S(1)} all-reduce(f32[512]{0:T(512)S(1)} %get-tuple-element.22), channel_id=1, replica_groups=mesh['img'=4,'ref'=8] {'ref'}, use_global_device_ids=true, to_apply=%region_1.0 | all-reduce | flops 512 | bytes 4096 | tf_op jit(solution)/shard_map/pmax | solution.py:37
  99.1 11.8 %psum.14 = f32[512]{0:T(512)S(1)} all-reduce(f32[512]{0:T(512)S(1)} %fusion.1), channel_id=1, replica_groups=mesh['img'=4,'ref'=8] {'ref'}, use_global_device_ids=true, to_apply=%region_3.0 | all-reduce | flops 512 | bytes 4096 | tf_op jit(solution)/shard_map/psum | solution.py:38
  111.4 17.6 %fusion.2 = f32[864,9216]{1,0:T(8,128)} fusion(bf16[512,864]{0,1:T(8,128)(2,1)S(1)} %get-tuple-element.3, bf16[512,9216]{1,0:T(8,128)(2,1)} %all-gather.2.cloned.1.call-done), kind=kOutput, calls=%fused_computation.44 | convolution fusion | flops 8153726976 | bytes 42172416 | tf_op jit(solution)/shard_map/dot_general | solution.py:44
  129.2 12.4 %psum.15 = f32[24]{0:T(128)} all-reduce(f32[24]{0:T(128)S(1)} %reduce_sum.29), channel_id=1, replica_groups=mesh['img'=4,'ref'=8] {'img'}, use_global_device_ids=true, to_apply=%region_7.0 | all-reduce | flops 24 | bytes 192 | tf_op jit(solution)/shard_map/psum | solution.py:43
  141.6 513.8 %reduce-scatter.2.cloned.1.call-done = f32[864,2304]{1,0:T(8,128)} async-done(((f32[864,9216]{1,0:T(8,128)}), f32[864,2304]{1,0:T(8,128)}) %reduce-scatter.2.cloned.1.call-update) | async-done | bytes 7962640 | tf_op jit(solution)/shard_map/reduce_scatter | solution.py:47
  655.4 15.2 %reshape_reshape.3 = f32[24,36,16,144]{3,2,1,0:T(8,128)} reshape(f32[864,2304]{1,0:T(8,128)} %reduce-scatter.2.cloned.1.call-done) | data formatting | bytes 15925248 | tf_op jit(solution)/shard_map/reshape;reshape | solution.py:11
  670.6 8.5 %maximum_add_fusion = f32[24,1,16,144]{3,2,1,0:T(8,128)} fusion(f32[24,36,16,144]{3,2,1,0:T(8,128)} %reshape_reshape.3), kind=kLoop, calls=%fused_computation.26 | loop fusion | flops 1769472 | bytes 14770176 | tf_op jit(solution)/shard_map/add | solution.py:16
  680.2 3.5 pad_maximum_fusion.18
  683.7 2.5 pad_maximum_fusion.17
  686.2 1.9 reshape.71
  688.1 1.9 squeeze.128
  690.0 1.9 squeeze.111
  691.9 1.9 squeeze.110
  693.8 1.9 squeeze.126
  695.6 1.9 squeeze.118
  697.5 1.9 squeeze.122
  699.4 1.9 squeeze.117
  701.3 1.9 squeeze.124
  703.2 1.9 squeeze.116
  705.1 1.9 squeeze.121
  709.5 2.7 add_add_fusion
  (24 shorter events, 6.4 us)
Async XLA Ops:
  7.2 64.3 %all-gather.2.cloned.1.call-start = ((), (), s32[]{:S(2)}) async-start(), calls=%async_computation.1 | async-start | bytes 10616832 | tf_op jit(solution)/shard_map/all_gather | solution.py:31
  7.9 647.5 %reduce-scatter.2.cloned.1.call-start = ((), (), s32[]{:S(2)}) async-start(), calls=%async_computation.2 | async-start | bytes 39813120 | tf_op jit(solution)/shard_map/reduce_scatter | solution.py:47
  670.6 8.6 %copy-start = (f32[24,36,16,144]{3,2,1,0:T(8,128)S(1)}, f32[24,36,16,144]{3,2,1,0:T(8,128)}, u32[]{:S(2)}) copy-start(f32[24,36,16,144]{3,2,1,0:T(8,128)} %reshape_reshape.3) | copy-start | bytes 23887876
Sparse Core Ops, SparseCore 0:
  9.9 61.5 all-gather.1
  129.1 526.1 reduce-scatter.1
where the time goes:
time: 720 us; the launch traced here: 719 us
  waiting for transfers between devices  570 us (79%)
  local copies, waits for them, and re-layouts  39.7 us (6%)
  blocking collectives  37.3 us (5%)
  matrix products  31.7 us (4%)
  other arithmetic  26.1 us (4%)
  between operations  14.1 us (2%)
    reduce_scatter x1, waiting for transfers between devices, per_device(): reduced = lax.psum_scatter(sums, 'img', scatter_dimension=1, tiled=True)  514 us
    all_gather x1, waiting for transfers between devices, per_device(): gathered = lax.all_gather(images, 'ref', axis=0, tiled=True)  55.7 us
    squeeze x19, local copies, waits for them, and re-layouts, unturn(): result = result + doubled[:, turn_index, :, start_col:start_col + ANG]  21.4 us
    dot_general x1, matrix products, per_device(): lax.dot_general(weights, gathered, (((0,), (0,)), ((), ())), preferred_el...  17.6 us
    another operation x1, local copies, waits for them, and re-layouts, unturn(): cycles = stacked.reshape(classes_here, rotations, columns // ANG, ANG)  15.2 us
  transfers between devices with their start and end apart: 2, of which 2 were waited for; matrix products, arithmetic and copies ran while one was open for 1% of the time, Pallas kernels for 0%

commit v1 on v0

--- a/solution.py
+++ b/solution.py
@@ -28,7 +28,17 @@
     offsets = (jnp.log(class_prior)[:, None] - half_norm.reshape(classes_here, rotations)).reshape(
         local_refs
     )
-    gathered = lax.all_gather(images, "ref", axis=0, tiled=True)
+    piece_next = jax.lax.axis_index("ref")
+    latest = jax.lax.axis_size("ref")
+    upper, h_now, local_now = (latest, piece_next, images.shape[0])
+    y_new, big = (images, 1)
+    while big < upper:
+        tile_out = jax.lax.ppermute(
+            y_new, "ref", tuple(((d, (d - big) % upper) for d in range(upper)))
+        )
+        y_new = jnp.concatenate([y_new, tile_out], axis=0)
+        big = 2 * big
+    gathered = jnp.roll(y_new, h_now * local_now, axis=0)
     products = lax.dot_general(
         gathered, references, (((1,), (1,)), ((), ())), preferred_element_type=jnp.float32
     )

time: 720 us -> 850 us (1.18)
  waiting for transfers between devices: 570 us -> 672 us
  local copies, waits for them, and re-layouts: 39.7 us -> 56.4 us
    ppermute x0 -> x3, waiting for transfers between devices: none -> 159 us  [per_device(): jax.lax.ppermute(y_new, 'ref', tuple(((d, (d - big) % upper) for d in ran...]
    all_gather x1 -> x0, waiting for transfers between devices: 55.7 us -> none  [per_device(): gathered = lax.all_gather(images, 'ref', axis=0, tiled=True)]
    unnamed x2 -> x25, local copies, waits for them, and re-layouts: 0.17 us -> 12.6 us
  transfers between devices with their start and end apart: 2 -> 4, of which waited for: 2 -> 4; matrix products, arithmetic and copies ran while one was open for 1% -> 1% of each run, Pallas kernels for 0% -> 0%
where the time goes in v1:
time: 850 us; the launch traced here: 849 us
  waiting for transfers between devices  672 us (79%)
  local copies, waits for them, and re-layouts  56.4 us (7%)
  blocking collectives  37.4 us (4%)
  other arithmetic  34.4 us (4%)
  matrix products  29.7 us (3%)
  between operations  14.1 us (2%)
    reduce_scatter x1, waiting for transfers between devices, per_device(): reduced = lax.psum_scatter(sums, 'img', scatter_dimension=1, tiled=True)  513 us
    ppermute x3, waiting for transfers between devices, per_device(): jax.lax.ppermute(y_new, 'ref', tuple(((d, (d - big) % upper) for d in ran...  159 us
    squeeze x19, local copies, waits for them, and re-layouts, unturn(): result = result + doubled[:, turn_index, :, start_col:start_col + ANG]  21.4 us
    dot_general x1, matrix products, per_device(): lax.dot_general(weights, gathered, (((0,), (0,)), ((), ())), preferred_el...  17.7 us
  transfers between devices with their start and end apart: 4, of which 4 were waited for; matrix products, arithmetic and copies ran while one was open for 1% of the time, Pallas kernels for 0%

profile of v1, /device:TPU:0, one launch (start us, length us, event | category | flops | bytes accessed | tf_op | source)
XLA Modules:
  0.0 848.6 jit_solution(8967913834083940004)
XLA Ops:
  7.2 3.4 collective-permute-start
  10.6 14.0 %collective-permute-done = bf16[64,9216]{1,0:T(8,128)(2,1)S(1)} collective-permute-done((bf16[64,9216]{1,0:T(8,128)(2,1)}, bf16[64,9216]{1,0:T(8,128)(2,1)S(1)}, u32[]{:S(2)}, u32[]{:S(2)}) %collective-permute-start) | collective-permute-done | bytes 1179680 | tf_op jit(solution)/shard_map/ppermute | solution.py:36
  27.1 53.0 %collective-permute-done.1 = bf16[128,9216]{1,0:T(8,128)(2,1)S(1)} collective-permute-done((bf16[128,9216]{1,0:T(8,128)(2,1)S(1)}, bf16[128,9216]{1,0:T(8,128)(2,1)S(1)}, u32[]{:S(2)}, u32[]{:S(2)}) %collective-permute-start.1) | collective-permute-done | bytes 2359328 | tf_op jit(solution)/shard_map/ppermute | solution.py:36
  80.1 3.4 pad_maximum_fusion
  84.4 7.1 fusion
  95.4 91.8 %collective-permute-done.2 = bf16[256,9216]{1,0:T(8,128)(2,1)} collective-permute-done((bf16[256,9216]{1,0:T(8,128)(2,1)}, bf16[256,9216]{1,0:T(8,128)(2,1)}, u32[]{:S(2)}, u32[]{:S(2)}) %collective-permute-start.2) | collective-permute-done | bytes 4718624 | tf_op jit(solution)/shard_map/ppermute | solution.py:36
  187.2 4.8 constant_dynamic-update-slice_fusion.4
  195.8 4.9 constant_dynamic-update-slice_fusion
  200.7 12.0 %add_reduce_fusion = (f32[512]{0:T(512)S(1)}, f32[512,864]{0,1:T(8,128)}) fusion(f32[864]{0:T(1024)S(1)} %multiply_subtract_fusion, bf16[864,9216]{1,0:T(8,128)(2,1)S(1)} %bitcast.43, bf16[1024,9216]{1,0:T(8,128)(2,1)} %constant_dynamic-update-slice_fusion, s32[]{:T(128)S(6)} %select_n.14), kind=kOutput, calls=%fused_computation.11 | convolution fusion | flops 8154611200 | bytes 27137412 | tf_op jit(solution)/shard_map/dot_general | solution.py:42
  212.7 13.0 %pmax.7 = f32[512]{0:T(512)S(1)} all-reduce(f32[512]{0:T(512)S(1)} %get-tuple-element.22), channel_id=1, replica_groups=mesh['img'=4,'ref'=8] {'ref'}, use_global_device_ids=true, to_apply=%region_1.2 | all-reduce | flops 512 | bytes 4096 | tf_op jit(solution)/shard_map/pmax | solution.py:47
  227.5 11.8 %psum.14 = f32[512]{0:T(512)S(1)} all-reduce(f32[512]{0:T(512)S(1)} %fusion.5), channel_id=1, replica_groups=mesh['img'=4,'ref'=8] {'ref'}, use_global_device_ids=true, to_apply=%region_3.4 | all-reduce | flops 512 | bytes 4096 | tf_op jit(solution)/shard_map/psum | solution.py:48
  239.3 2.0 convert_reduce_fusion
  241.3 17.7 %fusion.1 = f32[864,9216]{1,0:T(8,128)} fusion(bf16[512,864]{0,1:T(8,128)(2,1)S(1)} %get-tuple-element.3, bf16[1024,9216]{1,0:T(8,128)(2,1)} %constant_dynamic-update-slice_fusion, s32[]{:T(128)S(6)} %select_n.14), kind=kOutput, calls=%fused_computation.2 | convolution fusion | flops 8153726976 | bytes 42172420 | tf_op jit(solution)/shard_map/dot_general | solution.py:54
  259.3 12.6 %psum.15 = f32[24]{0:T(128)} all-reduce(f32[24]{0:T(128)S(1)} %reduce_sum.29), channel_id=1, replica_groups=mesh['img'=4,'ref'=8] {'img'}, use_global_device_ids=true, to_apply=%region_7.8 | all-reduce | flops 24 | bytes 192 | tf_op jit(solution)/shard_map/psum | solution.py:53
  271.9 513.0 %reduce-scatter.2.cloned.1.call-done = f32[864,2304]{1,0:T(8,128)} async-done(((f32[864,9216]{1,0:T(8,128)}), f32[864,2304]{1,0:T(8,128)}) %reduce-scatter.2.cloned.1.call-update) | async-done | bytes 7962640 | tf_op jit(solution)/shard_map/reduce_scatter | solution.py:57
  784.9 15.2 %reshape_reshape.3 = f32[24,36,16,144]{3,2,1,0:T(8,128)} reshape(f32[864,2304]{1,0:T(8,128)} %reduce-scatter.2.cloned.1.call-done) | data formatting | bytes 15925248 | tf_op jit(solution)/shard_map/reshape;reshape | solution.py:11
  800.2 8.5 maximum_add_fusion
  809.8 3.5 pad_maximum_fusion.20
  813.2 2.5 pad_maximum_fusion.19
  815.7 1.9 reshape.71
  819.5 1.9 squeeze.111
  828.9 1.9 squeeze.117
  832.7 1.9 squeeze.116
  839.1 2.7 add_add_fusion
  (54 shorter events, 30.0 us)
Async XLA Ops:
  7.2 77.1 %copy-start.4 = (f32[24]{0:T(128)S(1)}, f32[24]{0:T(128)}, u32[]{:S(2)}) copy-start(f32[24]{0:T(128)} %param.5) | copy-start | bytes 292
  7.2 777.7 %reduce-scatter.2.cloned.1.call-start = ((), (), s32[]{:S(2)}) async-start(), calls=%async_computation.1 | async-start | bytes 39813120 | tf_op jit(solution)/shard_map/reduce_scatter | solution.py:57
  7.2 17.4 %collective-permute-start = (bf16[64,9216]{1,0:T(8,128)(2,1)}, bf16[64,9216]{1,0:T(8,128)(2,1)S(1)}, u32[]{:S(2)}, u32[]{:S(2)}) collective-permute-start(bf16[64,9216]{1,0:T(8,128)(2,1)} %param.3), channel_id=1, source_target_pairs={{0,7},{1,0},{2,1},{3,2},{4,3},{5,4},{6,5},{7,6},{8,15},{9,8},{10,9... | collective-permute-start | bytes 3538952 | tf_op jit(solution)/shard_map/ppermute | solution.py:36
  24.6 55.5 %copy-start.2 = (bf16[64,9216]{1,0:T(8,128)(2,1)}, bf16[64,9216]{1,0:T(8,128)(2,1)S(1)}, u32[]{:S(2)}) copy-start(bf16[64,9216]{1,0:T(8,128)(2,1)S(1)} %collective-permute-done) | copy-start | bytes 3538948
  26.5 53.6 %collective-permute-start.1 = (bf16[128,9216]{1,0:T(8,128)(2,1)S(1)}, bf16[128,9216]{1,0:T(8,128)(2,1)S(1)}, u32[]{:S(2)}, u32[]{:S(2)}) collective-permute-start(bf16[128,9216]{1,0:T(8,128)(2,1)S(1)} %pad_maximum_fusion.1), channel_id=1, source_target_pairs={{0,6},{1,7},{2,0},{3,1},{4,2},{5,3},{6,4},{7,5},{8,14},{9,15},{10,... | collective-permute-start | bytes 7077896 | tf_op jit(solution)/shard_map/ppermute | solution.py:36
  83.5 8.0 copy-start.1
  83.5 103.6 %collective-permute-start.2 = (bf16[256,9216]{1,0:T(8,128)(2,1)}, bf16[256,9216]{1,0:T(8,128)(2,1)}, u32[]{:S(2)}, u32[]{:S(2)}) collective-permute-start(bf16[256,9216]{1,0:T(8,128)(2,1)} %pad_maximum_fusion), channel_id=1, source_target_pairs={{0,4},{1,5},{2,6},{3,7},{4,0},{5,1},{6,2},{7,3},{8,12},{9,13},{10,... | collective-permute-start | bytes 14155784 | tf_op jit(solution)/shard_map/ppermute | solution.py:36
  84.4 8.3 copy-start.3
  93.8 106.8 %slice-start = ((s8[15925248]{0:T(1024)(128)(4,1)}), s8[4194304]{0:T(1024)(128)(4,1)S(1)}, s32[]{:S(2)}) async-start(s8[15925248]{0:T(1024)(128)(4,1)} %bitcast.42), calls=%async_computation.2 | async-start | bytes 8388608
  95.4 105.3 %slice-start.1 = ((s8[15925248]{0:T(1024)(128)(4,1)}), s8[4194304]{0:T(1024)(128)(4,1)S(1)}, s32[]{:S(2)}) async-start(s8[15925248]{0:T(1024)(128)(4,1)} %bitcast.42), calls=%async_computation.3 | async-start | bytes 8388608
  193.1 7.6 slice-start.2
  195.8 4.9 slice-start.3
  800.2 8.6 %copy-start = (f32[24,36,16,144]{3,2,1,0:T(8,128)S(1)}, f32[24,36,16,144]{3,2,1,0:T(8,128)}, u32[]{:S(2)}) copy-start(f32[24,36,16,144]{3,2,1,0:T(8,128)} %reshape_reshape.3) | copy-start | bytes 23887876
Sparse Core Ops, SparseCore 0:
  259.2 525.6 reduce-scatter.1
